TPU v7x, 256 devices: a whole 4x4x8 slice. The times are simulated.
256 devices in a mesh: band: 16 (over z_hi, y, core), grid: 16 (over x, z_lo).
Axes of the slice: x: 4, y: 4, z: 8 (z_hi: 2, z_lo: 4; z = z_hi * 4 + z_lo), core: 2. Of those that a mesh axis runs over, the one named last changes fastest.
Arguments:
- bands: float32 [16, 2, 128, 128, 128], P('band', None, 'grid'), may hold values from -6 to 6
- coulomb: float32 [128, 128, 128], P(None, 'grid'), may hold values from 0.1 to 10
Outputs:
- exchange: float32 [16, 2, 128, 128, 128], P('band', None, 'grid')
All inputs are finite; a program needn't handle non-finite values.
Results may differ from a plain program's by a relative error of at most 0.0001.
Values sent between devices are 32-bit elements; how exact they have to be, the bound alone decides.
No kernel may reach another device: no remote copies, remote signals or barrier semaphores. Data moves between devices by JAX's collectives and lax.ppermute only.
A program may use at most 64 MiB of HBM per device.

v0:
```python
import math
import jax
import jax.numpy as jnp
from jax import lax
from jax.sharding import PartitionSpec as P

NX = 128
NY = 128
NZ = 128
STEPS = 2
einsum_forms = {1: "pnbc,nk->pkbc", 2: "panc,nk->pakc", 3: "pabn,nk->pabk"}


def from_root(value, axis, source):
    kept = jnp.where(lax.axis_index(axis) == source, value, 0).astype(value.dtype)
    return lax.psum(kept, axis)


def dft_tables(length):
    indices = jnp.arange(length, dtype=jnp.int32)
    products = indices[:, None] * indices[None, :] % length
    angles = products.astype(jnp.float32) * (2.0 * math.pi / length)
    return (jnp.cos(angles), jnp.sin(angles))


def transform(real_part, imag_part, axis_dim, inverse):
    cosine, sine_table = dft_tables(real_part.shape[axis_dim])
    form = einsum_forms[axis_dim]

    def contract(values, table):
        return jnp.einsum(form, values, table, precision=lax.Precision.HIGHEST)

    re_cos = contract(real_part, cosine)
    re_sin = contract(real_part, sine_table)
    im_cos = contract(imag_part, cosine)
    im_sin = contract(imag_part, sine_table)
    if inverse:
        return (re_cos - im_sin, im_cos + re_sin)
    return (re_cos + im_sin, im_cos - re_sin)


def body(bands, coulomb):
    local = bands.shape[0]
    groups = lax.axis_size("band")
    kernel = coulomb * (1.0 / (NX * NY * NZ))
    own_re = bands[:, 0]
    own_im = bands[:, 1]
    totals = (jnp.zeros_like(own_re), jnp.zeros_like(own_im))
    for step_index in range(STEPS):
        owner = step_index * groups // STEPS
        visitors = from_root(bands, "band", owner)
        pair_vis_re = visitors[:, 0]
        pair_vis_im = visitors[:, 1]
        pair_real_part = pair_vis_re[None] * own_re[:, None] + pair_vis_im[None] * own_im[:, None]
        pair_imag_part = pair_vis_re[None] * own_im[:, None] - pair_vis_im[None] * own_re[:, None]
        pair_shape = (local * local,) + pair_real_part.shape[2:]
        real_part = pair_real_part.reshape(pair_shape)
        imag_part = pair_imag_part.reshape(pair_shape)
        potentials_real_part = real_part
        potentials_imag_part = imag_part
        potentials_real_part, potentials_imag_part = transform(
            potentials_real_part, potentials_imag_part, 3, False
        )
        potentials_real_part, potentials_imag_part = transform(
            potentials_real_part, potentials_imag_part, 2, False
        )
        stacked = jnp.stack([potentials_real_part, potentials_imag_part], axis=1)
        block = lax.all_to_all(stacked, "grid", split_axis=3, concat_axis=2, tiled=True)
        pencil_real_part, pencil_imag_part = transform(block[:, 0], block[:, 1], 1, False)
        pencil_real_part = pencil_real_part * kernel[None]
        pencil_imag_part = pencil_imag_part * kernel[None]
        pencil_real_part, pencil_imag_part = transform(pencil_real_part, pencil_imag_part, 1, True)
        back = jnp.stack([pencil_real_part, pencil_imag_part], axis=1)
        result = lax.all_to_all(back, "grid", split_axis=2, concat_axis=3, tiled=True)
        potentials_real_part, potentials_imag_part = transform(result[:, 0], result[:, 1], 2, True)
        pot_re, pot_im = transform(potentials_real_part, potentials_imag_part, 3, True)
        accumulate_pot_re = pot_re
        accumulate_pot_im = pot_im
        vis_re = visitors[:, 0][None]
        vis_im = visitors[:, 1][None]
        shape = (local, local) + accumulate_pot_re.shape[1:]
        accumulate_pot_re = accumulate_pot_re.reshape(shape)
        accumulate_pot_im = accumulate_pot_im.reshape(shape)
        add_re = jnp.sum(accumulate_pot_re * vis_re - accumulate_pot_im * vis_im, axis=1)
        add_im = jnp.sum(accumulate_pot_re * vis_im + accumulate_pot_im * vis_re, axis=1)
        totals = (totals[0] + add_re, totals[1] + add_im)
    return -0.25 * jnp.stack([totals[0], totals[1]], axis=1)


def solution(mesh):
    in_specs = (P("band", None, "grid", None, None), P(None, "grid", None))
    out_specs = P("band", None, "grid", None, None)
    return jax.shard_map(body, mesh=mesh, in_specs=in_specs, out_specs=out_specs, check_vma=False)
```

profile of v0, /device:TPU:24, one launch (start us, length us, event | category | flops | bytes accessed | tf_op | source)
XLA Modules:
  0.0 357.9 jit_solution(3360302418520842808)
XLA Ops:
  6.5 2.8 broadcast_select_fusion.1
  9.3 185.8 %all-reduce.3.cloned.1.call-done = (f32[1,2,8,128,128]{4,3,2,1,0:T(8,128)}, f32[1,2,8,128,128]{4,3,2,1,0:T(8,128)}) async-done(((f32[1,2,8,128,128]{4,3,2,1,0:T(8,128)}, f32[1,2,8,128,128]{4,3,2,1,0:T(8,128)}), (f32[1,2,8,128,128]{4,3,2,1,0:T(8,128)}, f32[1,2,8,128,128]{4,3,2,1,0:T(8,128)})) %all-reduce.3.cloned.1.call-update) | async-done | bytes 2097168 | tf_op jit(solution)/shard_map/psum | solution.py:16
  195.1 1.8 multiply_add_fusion.1
  203.8 1.6 copy.44
  205.3 5.6 %all-to-all-start = ((f32[1,2,8,128,128]{4,2,1,0,3:T(8,128)}), f32[1,2,8,128,128]{4,2,1,0,3:T(8,128)S(1)}, u32[]{:S(2)}, u32[]{:S(2)}) async-start(f32[1,2,8,128,128]{4,2,1,0,3:T(8,128)} %copy.44), calls=%async_computation | async-start | bytes 2097152 | tf_op jit(solution)/shard_map/all_to_all | solution.py:68
  217.9 1.6 copy.65
  219.4 19.5 %all-to-all-done = f32[1,2,8,128,128]{4,2,1,0,3:T(8,128)S(1)} async-done(((f32[1,2,8,128,128]{4,2,1,0,3:T(8,128)}), f32[1,2,8,128,128]{4,2,1,0,3:T(8,128)S(1)}, u32[]{:S(2)}, u32[]{:S(2)}) %all-to-all-start) | async-done | bytes 1048608 | tf_op jit(solution)/shard_map/all_to_all | solution.py:68
  238.9 3.8 %all-to-all-start.2 = ((f32[1,2,8,128,128]{4,2,1,0,3:T(8,128)}), f32[1,2,8,128,128]{4,2,1,0,3:T(8,128)S(1)}, u32[]{:S(2)}, u32[]{:S(2)}) async-start(f32[1,2,8,128,128]{4,2,1,0,3:T(8,128)} %copy.65), calls=%async_computation.2 | async-start | bytes 2097152 | tf_op jit(solution)/shard_map/all_to_all | solution.py:68
  244.8 0.9 fusion.16
  246.6 0.9 fusion.17
  250.3 1.6 copy.55
  251.8 20.1 %all-to-all-done.2 = f32[1,2,8,128,128]{4,2,1,0,3:T(8,128)S(1)} async-done(((f32[1,2,8,128,128]{4,2,1,0,3:T(8,128)}), f32[1,2,8,128,128]{4,2,1,0,3:T(8,128)S(1)}, u32[]{:S(2)}, u32[]{:S(2)}) %all-to-all-start.2) | async-done | bytes 1048608 | tf_op jit(solution)/shard_map/all_to_all | solution.py:68
  271.9 3.9 %all-to-all-start.1 = ((f32[1,2,128,8,128]{4,3,1,0,2:T(8,128)}), f32[1,2,128,8,128]{4,3,1,0,2:T(8,128)S(1)}, u32[]{:S(2)}, u32[]{:S(2)}) async-start(f32[1,2,128,8,128]{4,3,1,0,2:T(8,128)} %copy.55), calls=%async_computation.1 | async-start | bytes 2097152 | tf_op jit(solution)/shard_map/all_to_all | solution.py:74
  277.6 0.9 fusion.6
  279.4 0.9 fusion.7
  282.1 0.9 fusion.5
  283.1 1.6 copy.75
  284.7 19.4 %all-to-all-done.1 = f32[1,2,128,8,128]{4,3,1,0,2:T(8,128)S(1)} async-done(((f32[1,2,128,8,128]{4,3,1,0,2:T(8,128)}), f32[1,2,128,8,128]{4,3,1,0,2:T(8,128)S(1)}, u32[]{:S(2)}, u32[]{:S(2)}) %all-to-all-start.1) | async-done | bytes 1048608 | tf_op jit(solution)/shard_map/all_to_all | solution.py:74
  304.1 4.6 %all-to-all-start.3 = ((f32[1,2,128,8,128]{4,3,1,0,2:T(8,128)}), f32[1,2,128,8,128]{4,3,1,0,2:T(8,128)}, u32[]{:S(2)}, u32[]{:S(2)}) async-start(f32[1,2,128,8,128]{4,3,1,0,2:T(8,128)} %copy.75), calls=%async_computation.3 | async-start | bytes 2097152 | tf_op jit(solution)/shard_map/all_to_all | solution.py:74
  310.5 25.1 %all-to-all-done.3 = f32[1,2,128,8,128]{4,3,1,0,2:T(8,128)} async-done(((f32[1,2,128,8,128]{4,3,1,0,2:T(8,128)}), f32[1,2,128,8,128]{4,3,1,0,2:T(8,128)}, u32[]{:S(2)}, u32[]{:S(2)}) %all-to-all-start.3) | async-done | bytes 1048608 | tf_op jit(solution)/shard_map/all_to_all | solution.py:74
  335.6 1.3 copy.158
  345.4 0.9 fusion.3
  348.5 1.0 subtract_add_fusion
  349.5 1.1 maximum_multiply_fusion
  (58 shorter events, 36.0 us)
Async XLA Ops:
  6.5 188.6 %all-reduce.3.cloned.1.call-start = ((), (), s32[]{:S(2)}) async-start(), calls=%async_computation.4 | async-start | bytes 4194304 | tf_op jit(solution)/shard_map/psum | solution.py:16
  9.3 185.8 %copy-start.1 = (f32[1,2,8,128,128]{4,3,2,1,0:T(8,128)S(1)}, f32[1,2,8,128,128]{4,3,2,1,0:T(8,128)}, u32[]{:S(2)}) copy-start(f32[1,2,8,128,128]{4,3,2,1,0:T(8,128)} %param.2) | copy-start | bytes 3145732
  205.3 33.6 %all-to-all-start = ((f32[1,2,8,128,128]{4,2,1,0,3:T(8,128)}), f32[1,2,8,128,128]{4,2,1,0,3:T(8,128)S(1)}, u32[]{:S(2)}, u32[]{:S(2)}) async-start(f32[1,2,8,128,128]{4,2,1,0,3:T(8,128)} %copy.44), calls=%async_computation | async-start | bytes 2097152 | tf_op jit(solution)/shard_map/all_to_all | solution.py:68
  238.9 33.0 %all-to-all-start.2 = ((f32[1,2,8,128,128]{4,2,1,0,3:T(8,128)}), f32[1,2,8,128,128]{4,2,1,0,3:T(8,128)S(1)}, u32[]{:S(2)}, u32[]{:S(2)}) async-start(f32[1,2,8,128,128]{4,2,1,0,3:T(8,128)} %copy.65), calls=%async_computation.2 | async-start | bytes 2097152 | tf_op jit(solution)/shard_map/all_to_all | solution.py:68
  243.8 1.0 copy-start
  271.9 32.2 %all-to-all-start.1 = ((f32[1,2,128,8,128]{4,3,1,0,2:T(8,128)}), f32[1,2,128,8,128]{4,3,1,0,2:T(8,128)S(1)}, u32[]{:S(2)}, u32[]{:S(2)}) async-start(f32[1,2,128,8,128]{4,3,1,0,2:T(8,128)} %copy.55), calls=%async_computation.1 | async-start | bytes 2097152 | tf_op jit(solution)/shard_map/all_to_all | solution.py:74
  304.1 31.6 %all-to-all-start.3 = ((f32[1,2,128,8,128]{4,3,1,0,2:T(8,128)}), f32[1,2,128,8,128]{4,3,1,0,2:T(8,128)}, u32[]{:S(2)}, u32[]{:S(2)}) async-start(f32[1,2,128,8,128]{4,3,1,0,2:T(8,128)} %copy.75), calls=%async_computation.3 | async-start | bytes 2097152 | tf_op jit(solution)/shard_map/all_to_all | solution.py:74
  346.3 1.7 copy-start.3
  347.2 1.3 copy-start.2
Sparse Core Ops, SparseCore 0:
  10.0 185.0 all-reduce.2
where the time goes:
time: 364 us; the launch traced here: 358 us
  waiting for transfers between devices  270 us (74%)
  matrix products  41.2 us (11%)
  starting transfers between devices  17.9 us (5%)
  between operations  14.3 us (4%)
  local copies, waits for them, and re-layouts  8.56 us (2%)
  other arithmetic  5.95 us (2%)
    psum x1, waiting for transfers between devices, from_root(): return lax.psum(kept, axis)  186 us
    all_to_all x2, waiting for transfers between devices, body(): lax.all_to_all(back, 'grid', split_axis=2, concat_axis=3, tiled=True)  44.5 us
    dot_general x48, matrix products, contract(): return jnp.einsum(form, values, table, precision=lax.Precision.HIGHEST)  41.2 us
    all_to_all x2, waiting for transfers between devices, body(): lax.all_to_all(stacked, 'grid', split_axis=3, concat_axis=2, tiled=True)  39.6 us
    all_to_all x2, starting transfers between devices, body(): lax.all_to_all(stacked, 'grid', split_axis=3, concat_axis=2, tiled=True)  9.45 us
    all_to_all x2, starting transfers between devices, body(): lax.all_to_all(back, 'grid', split_axis=2, concat_axis=3, tiled=True)  8.46 us
  transfers between devices with their start and end apart: 5, of which 5 were waited for; matrix products, arithmetic and copies ran while one was open for 8% of the time, Pallas kernels for 0%

commit v1 on v0

--- a/solution.py
+++ b/solution.py
@@ -3,6 +3,7 @@
 import jax.numpy as jnp
 from jax import lax
 from jax.sharding import PartitionSpec as P
+from jax.lax import all_gather
 
 NX = 128
 NY = 128
@@ -11,9 +12,14 @@
 einsum_forms = {1: "pnbc,nk->pkbc", 2: "panc,nk->pakc", 3: "pabn,nk->pabk"}
 
 
+def turns_press(work_x, mesh_name):
+    y2 = all_gather(work_x, mesh_name)
+    return jnp.sum(y2, axis=0)
+
+
 def from_root(value, axis, source):
     kept = jnp.where(lax.axis_index(axis) == source, value, 0).astype(value.dtype)
-    return lax.psum(kept, axis)
+    return turns_press(kept, axis)
 
 
 def dft_tables(length):

time: 364 us -> 538 us (1.48)
  the two profiles are of different devices: /device:TPU:24 before, /device:TPU:1 now
where the time goes in v1:
time: 538 us; the launch traced here: 529 us
  waiting for transfers between devices  416 us (77%)
  matrix products  47 us (9%)
  other arithmetic  21.3 us (4%)
  starting transfers between devices  18.6 us (3%)
  between operations  14.3 us (3%)
  local copies, waits for them, and re-layouts  11.7 us (2%)
    all_gather x2, waiting for transfers between devices, turns_press(): y2 = all_gather(work_x, mesh_name)  342 us
    dot_general x48, matrix products, contract(): return jnp.einsum(form, values, table, precision=lax.Precision.HIGHEST)  47 us
    all_to_all x2, waiting for transfers between devices, body(): lax.all_to_all(back, 'grid', split_axis=2, concat_axis=3, tiled=True)  39.2 us
    all_to_all x2, waiting for transfers between devices, body(): lax.all_to_all(stacked, 'grid', split_axis=3, concat_axis=2, tiled=True)  33.6 us
    reduce_sum x2, other arithmetic, turns_press(): return jnp.sum(y2, axis=0)  14.8 us
  transfers between devices with their start and end apart: 6, of which 6 were waited for; matrix products, arithmetic and copies ran while one was open for 8% of the time, Pallas kernels for 0%

profile of v1, /device:TPU:1, one launch (start us, length us, event | category | flops | bytes accessed | tf_op | source)
XLA Modules:
  0.0 528.8 jit_solution(11364402719707791951)
XLA Ops:
  6.5 2.8 broadcast_select_fusion.1
  10.1 178.4 %all-gather.5.cloned.1.call-done = f32[16,2,8,128,128]{4,3,2,1,0:T(8,128)} async-done(((f32[1,2,8,128,128]{4,3,2,1,0:T(8,128)}), f32[16,2,8,128,128]{4,3,2,1,0:T(8,128)}) %all-gather.5.cloned.1.call-update) | async-done | bytes 16777232 | tf_op jit(solution)/shard_map/all_gather | solution.py:16
  188.5 7.4 %reduce.2 = f32[2,8,128,128]{3,2,1,0:T(8,128)S(1)} reduce(f32[16,2,8,128,128]{4,3,2,1,0:T(8,128)} %all-gather.5.cloned.1.call-done, f32[]{:T(128)} %constant.61.clone.1), dimensions={0}, to_apply=%region_0.1 | reduce | flops 3932160 | bytes 17825796 | tf_op jit(solution)/shard_map/reduce_sum | solution.py:17
  195.9 164.0 %all-gather.7.cloned.1.call-done = f32[16,2,8,128,128]{4,3,2,1,0:T(8,128)} async-done(((f32[1,2,8,128,128]{4,3,2,1,0:T(8,128)}), f32[16,2,8,128,128]{4,3,2,1,0:T(8,128)}) %all-gather.7.cloned.1.call-update) | async-done | bytes 16777232 | tf_op jit(solution)/shard_map/all_gather | solution.py:16
  359.9 7.4 %reduce.3 = f32[2,8,128,128]{3,2,1,0:T(8,128)S(1)} reduce(f32[16,2,8,128,128]{4,3,2,1,0:T(8,128)} %all-gather.7.cloned.1.call-done, f32[]{:T(128)} %constant.61.clone.1), dimensions={0}, to_apply=%region_1.2 | reduce | flops 3932160 | bytes 17825796 | tf_op jit(solution)/shard_map/reduce_sum | solution.py:17
  367.3 2.3 multiply_add_fusion.1
  376.5 1.6 copy.44
  378.1 4.8 all-to-all-start
  382.9 1.9 fusion.20
  385.6 1.9 convolution_add_fusion.5
  391.9 1.6 copy.65
  393.5 16.7 %all-to-all-done = f32[1,2,8,128,128]{4,2,1,0,3:T(8,128)} async-done(((f32[1,2,8,128,128]{4,2,1,0,3:T(8,128)}), f32[1,2,8,128,128]{4,2,1,0,3:T(8,128)}, u32[]{:S(2)}, u32[]{:S(2)}) %all-to-all-start) | async-done | bytes 1048608 | tf_op jit(solution)/shard_map/all_to_all | solution.py:74
  410.2 4.5 all-to-all-start.2
  423.2 1.6 copy.55
  424.8 16.9 %all-to-all-done.2 = f32[1,2,8,128,128]{4,2,1,0,3:T(8,128)} async-done(((f32[1,2,8,128,128]{4,2,1,0,3:T(8,128)}), f32[1,2,8,128,128]{4,2,1,0,3:T(8,128)}, u32[]{:S(2)}, u32[]{:S(2)}) %all-to-all-start.2) | async-done | bytes 1048608 | tf_op jit(solution)/shard_map/all_to_all | solution.py:74
  441.7 4.6 all-to-all-start.1
  454.9 1.6 copy.75
  456.5 17.0 %all-to-all-done.1 = f32[1,2,128,8,128]{4,3,1,0,2:T(8,128)} async-done(((f32[1,2,128,8,128]{4,3,1,0,2:T(8,128)}), f32[1,2,128,8,128]{4,3,1,0,2:T(8,128)}, u32[]{:S(2)}, u32[]{:S(2)}) %all-to-all-start.1) | async-done | bytes 1048608 | tf_op jit(solution)/shard_map/all_to_all | solution.py:80
  473.4 4.7 all-to-all-start.3
  479.4 1.7 fusion.35
  481.1 1.7 fusion.34
  482.7 22.2 %all-to-all-done.3 = f32[1,2,128,8,128]{4,3,1,0,2:T(8,128)} async-done(((f32[1,2,128,8,128]{4,3,1,0,2:T(8,128)}), f32[1,2,128,8,128]{4,3,1,0,2:T(8,128)}, u32[]{:S(2)}, u32[]{:S(2)}) %all-to-all-start.3) | async-done | bytes 1048608 | tf_op jit(solution)/shard_map/all_to_all | solution.py:80
  508.0 1.9 fusion.12
  510.7 1.9 fusion.13
  (57 shorter events, 43.7 us)
Async XLA Ops:
  6.5 182.0 %all-gather.5.cloned.1.call-start = ((), (), s32[]{:S(2)}) async-start(), calls=%async_computation.4 | async-start | bytes 17825792 | tf_op jit(solution)/shard_map/all_gather | solution.py:16
  9.4 350.6 %all-gather.7.cloned.1.call-start = ((), (), s32[]{:S(2)}) async-start(), calls=%async_computation.5 | async-start | bytes 17825792 | tf_op jit(solution)/shard_map/all_gather | solution.py:16
  372.1 45.7 %copy-start = (f32[128,8,128]{2,1,0:T(8,128)S(1)}, f32[128,8,128]{2,1,0:T(8,128)}, u32[]{:S(2)}) copy-start(f32[128,8,128]{2,1,0:T(8,128)} %param.3) | copy-start | bytes 1572868
  378.1 32.0 %all-to-all-start = ((f32[1,2,8,128,128]{4,2,1,0,3:T(8,128)}), f32[1,2,8,128,128]{4,2,1,0,3:T(8,128)}, u32[]{:S(2)}, u32[]{:S(2)}) async-start(f32[1,2,8,128,128]{4,2,1,0,3:T(8,128)} %copy.44), calls=%async_computation | async-start | bytes 2097152 | tf_op jit(solution)/shard_map/all_to_all | solution.py:74
  410.2 31.6 %all-to-all-start.2 = ((f32[1,2,8,128,128]{4,2,1,0,3:T(8,128)}), f32[1,2,8,128,128]{4,2,1,0,3:T(8,128)}, u32[]{:S(2)}, u32[]{:S(2)}) async-start(f32[1,2,8,128,128]{4,2,1,0,3:T(8,128)} %copy.65), calls=%async_computation.2 | async-start | bytes 2097152 | tf_op jit(solution)/shard_map/all_to_all | solution.py:74
  441.7 31.7 %all-to-all-start.1 = ((f32[1,2,128,8,128]{4,3,1,0,2:T(8,128)}), f32[1,2,128,8,128]{4,3,1,0,2:T(8,128)}, u32[]{:S(2)}, u32[]{:S(2)}) async-start(f32[1,2,128,8,128]{4,3,1,0,2:T(8,128)} %copy.55), calls=%async_computation.1 | async-start | bytes 2097152 | tf_op jit(solution)/shard_map/all_to_all | solution.py:80
  473.4 31.5 %all-to-all-start.3 = ((f32[1,2,128,8,128]{4,3,1,0,2:T(8,128)}), f32[1,2,128,8,128]{4,3,1,0,2:T(8,128)}, u32[]{:S(2)}, u32[]{:S(2)}) async-start(f32[1,2,128,8,128]{4,3,1,0,2:T(8,128)} %copy.75), calls=%async_computation.3 | async-start | bytes 2097152 | tf_op jit(solution)/shard_map/all_to_all | solution.py:80
Sparse Core Ops, SparseCore 0:
  10.1 178.4 all-gather.4
  191.3 168.6 all-gather.6
